TPU v7x, 512 devices: a whole 4x8x8 slice. The times are simulated.
512 devices in a mesh: grid: 64 (over x, z, core), orb: 8 (over y).
Axes of the slice: x: 4, y: 8, z: 8, core: 2. Of those that a mesh axis runs over, the one named last changes fastest.
Arguments:
- orbitals: float32 [256, 16, 16, 1024], P('grid', None, None, 'orb'), may hold values from -15 to 15
- potential: float32 [256, 16, 16], P('grid'), may hold values from -2 to 0
Outputs:
- filtered: float32 [256, 16, 16, 1024], P('grid', None, None, 'orb')
- hamiltonian_block: float32 [1024, 1024], P('orb', 'grid')
- margin_block: float32 [1024, 1024], P('orb', 'grid')
All inputs are finite; a program needn't handle non-finite values.
Results may differ from a plain program's by a relative error of at most 0.0039.
Values may be sent and summed in bfloat16 or wider, within the bound.
No kernel may reach another device: no remote copies, remote signals or barrier semaphores. Data moves between devices by JAX's collectives and lax.ppermute only.
A program may use at most 64 MiB of HBM per device.

v0:
```python
import jax
import jax.numpy as jnp
from jax import lax
from jax.sharding import PartitionSpec as P

DEGREE = 4
STENCIL = (-205.0 / 72.0, 8.0 / 5.0, -1.0 / 5.0, 8.0 / 315.0, -1.0 / 560.0)
LOWER_EDGE = -2.0
CUT_EDGE = 1.5
UPPER_EDGE = 10.0
EPSILON = 1e-06


def halo_layers(shard, width):
    size = lax.axis_size("grid")
    length = shard.shape[0]
    up = [(i, i + 1) for i in range(size - 1)]
    down = [(j, i) for i, j in up]
    last = lax.slice_in_dim(shard, length - width, length, axis=0).astype(jnp.bfloat16)
    initial = lax.slice_in_dim(shard, 0, width, axis=0).astype(jnp.bfloat16)
    before = lax.ppermute(last, "grid", up).astype(shard.dtype)
    after = lax.ppermute(initial, "grid", down).astype(shard.dtype)
    return jnp.concatenate([before, shard, after], axis=0)


def plane_matrix(rows_y, cols_x):
    flat_count = rows_y * cols_x
    index_all = jnp.arange(flat_count, dtype=jnp.int32)
    row_y = (index_all // cols_x)[:, None]
    row_x = (index_all % cols_x)[:, None]
    col_y = (index_all // cols_x)[None, :]
    col_x = (index_all % cols_x)[None, :]
    delta_y = jnp.mod(row_y - col_y, rows_y)
    delta_x = jnp.mod(row_x - col_x, cols_x)
    same_y = delta_y == 0
    same_x = delta_x == 0
    matrix = jnp.zeros((flat_count, flat_count), jnp.float32)
    for offset in range(1, 5):
        for signed in (offset, -offset):
            hit_y = jnp.logical_and(same_x, delta_y == signed % rows_y)
            hit_x = jnp.logical_and(same_y, delta_x == signed % cols_x)
            matrix = matrix + STENCIL[offset] * (
                hit_y.astype(jnp.float32) + hit_x.astype(jnp.float32)
            )
    return matrix


def apply_hamiltonian(current, potential, plane):
    layers, rows_y, cols_x, width = current.shape
    padded = halo_layers(current, 4)
    laplacian = 3.0 * STENCIL[0] * current
    for offset in range(1, 5):
        laplacian = laplacian + STENCIL[offset] * (
            padded[4 + offset : 4 + offset + layers] + padded[4 - offset : 4 - offset + layers]
        )
    flat = current.reshape(layers, rows_y * cols_x, width)
    in_plane = jnp.einsum(
        "pq,zqo->zpo",
        plane,
        flat,
        precision=lax.Precision.HIGHEST,
        preferred_element_type=jnp.float32,
    )
    laplacian = laplacian + in_plane.reshape(current.shape)
    return -0.5 * laplacian + potential[:, :, :, None] * current


def chebyshev(initial, potential, plane):
    half_width = (UPPER_EDGE - CUT_EDGE) / 2.0
    centre = (UPPER_EDGE + CUT_EDGE) / 2.0
    sigma_now = half_width / (LOWER_EDGE - centre)
    gamma_ratio = 2.0 / sigma_now
    previous = initial
    current = (
        sigma_now / half_width * (apply_hamiltonian(previous, potential, plane) - centre * previous)
    )
    for degree_step in range(DEGREE - 1):
        sigma_next = 1.0 / (gamma_ratio - sigma_now)
        following = (
            2.0
            * sigma_next
            / half_width
            * (apply_hamiltonian(current, potential, plane) - centre * current)
            - sigma_now * sigma_next * previous
        )
        previous, current, sigma_now = (current, following, sigma_next)
    return current


def contract_points(left_side, right_side):
    return lax.dot_general(
        left_side, right_side, (((0,), (0,)), ((), ())), preferred_element_type=jnp.float32
    )


def reduce_scatter_grid(slots):
    size = slots.shape[0]
    bits = size.bit_length() - 1
    me = lax.axis_index("grid")
    rest = slots.shape[1:]
    buf = slots.reshape((2,) * bits + rest)
    for bit in range(bits):
        axis = bits - 1 - bit
        mine = me >> bit & 1
        low = lax.index_in_dim(buf, 0, axis=axis, keepdims=False)
        high = lax.index_in_dim(buf, 1, axis=axis, keepdims=False)
        keep = jnp.where(mine == 1, high, low)
        send = jnp.where(mine == 1, low, high)
        pairs = [(i, i ^ 1 << bit) for i in range(size)]
        buf = keep + lax.ppermute(send, "grid", pairs)
    return buf


def on_device(orbitals, potential):
    own_width = orbitals.shape[3]
    point_count = orbitals.shape[0] * orbitals.shape[1] * orbitals.shape[2]
    grid_size = lax.axis_size("grid")
    point_total = float(point_count * grid_size)
    plane = plane_matrix(orbitals.shape[1], orbitals.shape[2])
    result_block = chebyshev(orbitals, potential, plane)
    own_squares = jnp.sum(result_block * result_block, axis=(0, 1, 2))
    rounded_orbitals = result_block.astype(jnp.bfloat16).reshape(point_count, own_width)
    rounded_image = (
        apply_hamiltonian(result_block, potential, plane)
        .astype(jnp.bfloat16)
        .reshape(point_count, own_width)
    )
    orbitals_all = lax.all_gather(rounded_orbitals, "orb", axis=1, tiled=True)
    total_width = orbitals_all.shape[1]
    rows = total_width // grid_size
    hamiltonian_part = contract_points(orbitals_all, rounded_image)
    margin_part = contract_points(orbitals_all, rounded_orbitals)
    wide = orbitals_all.astype(jnp.float32)
    column_squares = jnp.sum(wide * wide, axis=0)
    body = jnp.concatenate(
        [
            hamiltonian_part.reshape(grid_size, rows, own_width),
            margin_part.reshape(grid_size, rows, own_width),
        ],
        axis=2,
    )
    tail = jnp.concatenate(
        [
            column_squares.reshape(grid_size, rows),
            jnp.broadcast_to(own_squares[None, :], (grid_size, own_width)),
            jnp.zeros((grid_size, own_width - rows), jnp.float32),
        ],
        axis=1,
    )
    slots = jnp.concatenate([body, tail[:, None, :]], axis=1)
    combined = reduce_scatter_grid(slots)
    scale_own = 1.0 / jnp.sqrt(combined[rows, rows : rows + own_width] / point_total + EPSILON)
    column_scale = 1.0 / jnp.sqrt(combined[rows, :rows] / point_total + EPSILON)
    filtered = result_block * scale_own
    pair_scale = scale_own[:, None] * column_scale[None, :] / point_total
    hamiltonian_block = combined[:rows, :own_width].T * pair_scale
    margin_block = combined[:rows, own_width:].T * pair_scale
    return (filtered, hamiltonian_block, margin_block)


def solution(mesh):
    placed = (P("grid", None, None, "orb"), P("grid", None, None))
    return jax.shard_map(
        on_device,
        mesh=mesh,
        in_specs=placed,
        out_specs=(P("grid", None, None, "orb"), P("orb", "grid"), P("orb", "grid")),
        check_vma=False,
    )
```

profile of v0, /device:TPU:2, one launch (start us, length us, event | category | flops | bytes accessed | tf_op | source)
XLA Modules:
  0.0 181.1 jit_solution(14058231074587495252)
XLA Ops:
  7.2 1.1 convert_element_type.233
  8.3 10.4 %collective-permute-start = (bf16[4,16,16,128]{3,2,1,0:T(8,128)(2,1)S(1)}, bf16[4,16,16,128]{3,2,1,0:T(8,128)(2,1)S(1)}, u32[]{:S(2)}, u32[]{:S(2)}) collective-permute-start(bf16[4,16,16,128]{3,2,1,0:T(8,128)(2,1)S(1)} %convert_element_type.233), channel_id=1, source_target_pairs={{8,0},{16,8},{24,16},{32,24},{40,32},{48,40},{56,48},{64,56},{72,6... | collective-permute-start | bytes 786440 | tf_op jit(solution)/shard_map/ppermute | solution.py:22
  18.7 1.9 %collective-permute-start.1 = (bf16[4,16,16,128]{3,2,1,0:T(8,128)(2,1)S(1)}, bf16[4,16,16,128]{3,2,1,0:T(8,128)(2,1)S(1)}, u32[]{:S(2)}, u32[]{:S(2)}) collective-permute-start(bf16[4,16,16,128]{3,2,1,0:T(8,128)(2,1)S(1)} %convert_element_type.233), channel_id=1, source_target_pairs={{0,8},{8,16},{16,24},{24,32},{32,40},{40,48},{48,56},{56,64},{64,7... | collective-permute-start | bytes 786440 | tf_op jit(solution)/shard_map/ppermute | solution.py:21
  20.6 0.8 broadcast_multiply_fusion.2
  21.4 2.7 %fusion.102 = f32[256,4,128]{2,0,1:T(8,128)S(1)} fusion(f32[4,256,128]{2,1,0:T(8,128)} %bitcast.96, s32[256]{0:T(256)S(1)} %get-tuple-element.22, s32[256]{0:T(256)S(1)} %get-tuple-element.23), kind=kOutput, calls=%fused_computation.176 | convolution fusion | flops 408944640 | bytes 1050624 | tf_op jit(solution)/shard_map/pq,zqo->zpo/dot_general | solution.py:57
  24.2 4.3 %collective-permute-done.1 = bf16[4,16,16,128]{3,2,1,0:T(8,128)(2,1)S(1)} collective-permute-done((bf16[4,16,16,128]{3,2,1,0:T(8,128)(2,1)S(1)}, bf16[4,16,16,128]{3,2,1,0:T(8,128)(2,1)S(1)}, u32[]{:S(2)}, u32[]{:S(2)}) %collective-permute-start.1) | collective-permute-done | bytes 262176 | tf_op jit(solution)/shard_map/ppermute | solution.py:21
  28.9 1.9 %collective-permute-start.2 = (bf16[4,16,16,128]{3,2,1,0:T(8,128)(2,1)S(1)}, bf16[4,16,16,128]{3,2,1,0:T(8,128)(2,1)S(1)}, u32[]{:S(2)}, u32[]{:S(2)}) collective-permute-start(bf16[4,16,16,128]{3,2,1,0:T(8,128)(2,1)S(1)} %get-tuple-element.9), channel_id=1, source_target_pairs={{8,0},{16,8},{24,16},{32,24},{40,32},{48,40},{56,48},{64,56},{72,6... | collective-permute-start | bytes 786440 | tf_op jit(solution)/shard_map/ppermute | solution.py:22
  30.8 2.4 %collective-permute-start.3 = (bf16[4,16,16,128]{3,2,1,0:T(8,128)(2,1)S(1)}, bf16[4,16,16,128]{3,2,1,0:T(8,128)(2,1)S(1)}, u32[]{:S(2)}, u32[]{:S(2)}) collective-permute-start(bf16[4,16,16,128]{3,2,1,0:T(8,128)(2,1)S(1)} %get-tuple-element.9), channel_id=1, source_target_pairs={{0,8},{8,16},{16,24},{24,32},{32,40},{40,48},{48,56},{56,64},{64,7... | collective-permute-start | bytes 786440 | tf_op jit(solution)/shard_map/ppermute | solution.py:21
  33.3 1.9 %convolution_bitcast_fusion.3 = f32[4,256,128]{1,2,0:T(8,128)S(1)} fusion(f32[4,256,128]{2,1,0:T(8,128)S(1)} %bitcast.101, s32[256]{0:T(256)S(1)} %get-tuple-element.22, s32[256]{0:T(256)S(1)} %get-tuple-element.23), kind=kOutput, calls=%fused_computation.44 | convolution fusion | flops 408944640 | bytes 1050624 | tf_op jit(solution)/shard_map/pq,zqo->zpo/dot_general | solution.py:57
  35.5 5.1 %collective-permute-done.3 = bf16[4,16,16,128]{3,2,1,0:T(8,128)(2,1)S(1)} collective-permute-done((bf16[4,16,16,128]{3,2,1,0:T(8,128)(2,1)S(1)}, bf16[4,16,16,128]{3,2,1,0:T(8,128)(2,1)S(1)}, u32[]{:S(2)}, u32[]{:S(2)}) %collective-permute-start.3) | collective-permute-done | bytes 262176 | tf_op jit(solution)/shard_map/ppermute | solution.py:21
  40.7 0.4 fusion.199
  41.1 1.9 %collective-permute-start.4 = (bf16[4,16,16,128]{3,2,1,0:T(8,128)(2,1)S(1)}, bf16[4,16,16,128]{3,2,1,0:T(8,128)(2,1)S(1)}, u32[]{:S(2)}, u32[]{:S(2)}) collective-permute-start(bf16[4,16,16,128]{3,2,1,0:T(8,128)(2,1)S(1)} %get-tuple-element.7), channel_id=1, source_target_pairs={{8,0},{16,8},{24,16},{32,24},{40,32},{48,40},{56,48},{64,56},{72,6... | collective-permute-start | bytes 786440 | tf_op jit(solution)/shard_map/ppermute | solution.py:22
  43.1 2.4 %collective-permute-start.5 = (bf16[4,16,16,128]{3,2,1,0:T(8,128)(2,1)S(1)}, bf16[4,16,16,128]{3,2,1,0:T(8,128)(2,1)S(1)}, u32[]{:S(2)}, u32[]{:S(2)}) collective-permute-start(bf16[4,16,16,128]{3,2,1,0:T(8,128)(2,1)S(1)} %get-tuple-element.7), channel_id=1, source_target_pairs={{0,8},{8,16},{16,24},{24,32},{32,40},{40,48},{48,56},{56,64},{64,7... | collective-permute-start | bytes 786440 | tf_op jit(solution)/shard_map/ppermute | solution.py:21
  45.5 1.9 %convolution_bitcast_fusion.2 = f32[4,256,128]{1,2,0:T(8,128)S(1)} fusion(f32[4,256,128]{2,1,0:T(8,128)S(1)} %bitcast.97, s32[256]{0:T(256)S(1)} %get-tuple-element.22, s32[256]{0:T(256)S(1)} %get-tuple-element.23), kind=kOutput, calls=%fused_computation.43 | convolution fusion | flops 408944640 | bytes 1050624 | tf_op jit(solution)/shard_map/pq,zqo->zpo/dot_general | solution.py:57
  47.7 5.2 %collective-permute-done.5 = bf16[4,16,16,128]{3,2,1,0:T(8,128)(2,1)S(1)} collective-permute-done((bf16[4,16,16,128]{3,2,1,0:T(8,128)(2,1)S(1)}, bf16[4,16,16,128]{3,2,1,0:T(8,128)(2,1)S(1)}, u32[]{:S(2)}, u32[]{:S(2)}) %collective-permute-start.5) | collective-permute-done | bytes 262176 | tf_op jit(solution)/shard_map/ppermute | solution.py:21
  53.3 1.9 %collective-permute-start.6 = (bf16[4,16,16,128]{3,2,1,0:T(8,128)(2,1)S(1)}, bf16[4,16,16,128]{3,2,1,0:T(8,128)(2,1)S(1)}, u32[]{:S(2)}, u32[]{:S(2)}) collective-permute-start(bf16[4,16,16,128]{3,2,1,0:T(8,128)(2,1)S(1)} %get-tuple-element.5), channel_id=1, source_target_pairs={{8,0},{16,8},{24,16},{32,24},{40,32},{48,40},{56,48},{64,56},{72,6... | collective-permute-start | bytes 786440 | tf_op jit(solution)/shard_map/ppermute | solution.py:22
  55.2 2.4 %collective-permute-start.7 = (bf16[4,16,16,128]{3,2,1,0:T(8,128)(2,1)S(1)}, bf16[4,16,16,128]{3,2,1,0:T(8,128)(2,1)S(1)}, u32[]{:S(2)}, u32[]{:S(2)}) collective-permute-start(bf16[4,16,16,128]{3,2,1,0:T(8,128)(2,1)S(1)} %get-tuple-element.5), channel_id=1, source_target_pairs={{0,8},{8,16},{16,24},{24,32},{32,40},{40,48},{48,56},{56,64},{64,7... | collective-permute-start | bytes 786440 | tf_op jit(solution)/shard_map/ppermute | solution.py:21
  57.7 1.9 %convolution_bitcast_fusion.1 = f32[4,256,128]{1,2,0:T(8,128)S(1)} fusion(f32[4,256,128]{2,1,0:T(8,128)S(1)} %bitcast.106, s32[256]{0:T(256)S(1)} %get-tuple-element.22, s32[256]{0:T(256)S(1)} %get-tuple-element.23), kind=kOutput, calls=%fused_computation.42 | convolution fusion | flops 408944640 | bytes 1050624 | tf_op jit(solution)/shard_map/pq,zqo->zpo/dot_general | solution.py:57
  59.8 5.2 %collective-permute-done.7 = bf16[4,16,16,128]{3,2,1,0:T(8,128)(2,1)S(1)} collective-permute-done((bf16[4,16,16,128]{3,2,1,0:T(8,128)(2,1)S(1)}, bf16[4,16,16,128]{3,2,1,0:T(8,128)(2,1)S(1)}, u32[]{:S(2)}, u32[]{:S(2)}) %collective-permute-start.7) | collective-permute-done | bytes 262176 | tf_op jit(solution)/shard_map/ppermute | solution.py:21
  65.1 0.5 multiply_reduce_fusion.1
  65.5 0.7 convert_element_type.261
  66.4 1.9 %collective-permute-start.9 = (bf16[4,16,16,128]{3,2,1,0:T(8,128)(2,1)}, bf16[4,16,16,128]{3,2,1,0:T(8,128)(2,1)S(1)}, u32[]{:S(2)}, u32[]{:S(2)}) collective-permute-start(bf16[4,16,16,128]{3,2,1,0:T(8,128)(2,1)} %convert_element_type.261), channel_id=1, source_target_pairs={{0,8},{8,16},{16,24},{24,32},{32,40},{40,48},{48,56},{56,64},{64,7... | collective-permute-start | bytes 786440 | tf_op jit(solution)/shard_map/ppermute | solution.py:21
  68.3 5.9 %collective-permute-start.8 = (bf16[4,16,16,128]{3,2,1,0:T(8,128)(2,1)}, bf16[4,16,16,128]{3,2,1,0:T(8,128)(2,1)S(1)}, u32[]{:S(2)}, u32[]{:S(2)}) collective-permute-start(bf16[4,16,16,128]{3,2,1,0:T(8,128)(2,1)} %convert_element_type.261), channel_id=1, source_target_pairs={{8,0},{16,8},{24,16},{32,24},{40,32},{48,40},{56,48},{64,56},{72,6... | collective-permute-start | bytes 786440 | tf_op jit(solution)/shard_map/ppermute | solution.py:22
  74.3 1.9 %convolution_bitcast_fusion = f32[4,256,128]{1,2,0:T(8,128)S(1)} fusion(f32[4,256,128]{2,1,0:T(8,128)S(1)} %bitcast.95, s32[256]{0:T(256)S(1)} %get-tuple-element.22, s32[256]{0:T(256)S(1)} %get-tuple-element.23), kind=kOutput, calls=%fused_computation.41 | convolution fusion | flops 408944640 | bytes 1050624 | tf_op jit(solution)/shard_map/pq,zqo->zpo/dot_general | solution.py:57
  76.5 1.7 collective-permute-done.8
  78.6 34.1 %all-gather.2.cloned.1.call-done = bf16[1024,1024]{1,0:T(8,128)(2,1)} async-done(((bf16[1024,128]{1,0:T(8,128)(2,1)}), bf16[1024,1024]{1,0:T(8,128)(2,1)}) %all-gather.2.cloned.1.call-update) | async-done | bytes 2097168 | tf_op jit(solution)/shard_map/all_gather | solution.py:128
  112.8 2.1 %multiply_reduce_fusion = f32[1024]{0:T(1024)S(1)} fusion(bf16[1024,1024]{1,0:T(8,128)(2,1)} %all-gather.2.cloned.1.call-done), kind=kLoop, calls=%fused_computation | loop fusion | flops 3144704 | bytes 2101248 | tf_op jit(solution)/shard_map/reduce_sum | solution.py:134
  115.0 2.9 %copy.191 = bf16[1024,1024]{1,0:T(8,128)(2,1)S(1)} copy(bf16[1024,1024]{0,1:T(8,128)(2,1)} %bitcast.94) | data formatting | bytes 4194304 | tf_op jit(solution)/shard_map/dot_general | solution.py:91
  117.9 0.7 fusion.204
  118.6 0.7 fusion.203
  119.4 0.8 copy.195
  120.3 0.6 maximum_maximum_fusion
  121.1 1.2 copy.196
  122.4 1.9 %collective-permute-start.10 = (f32[2,2,2,2,2,17,256]{6,4,5,3,2,1,0:T(2,128)}, f32[2,2,2,2,2,17,256]{6,4,5,3,2,1,0:T(2,128)S(1)}, u32[]{:S(2)}, u32[]{:S(2)}) collective-permute-start(f32[2,2,2,2,2,17,256]{6,4,5,3,2,1,0:T(2,128)} %copy.196), channel_id=1, source_target_pairs={{0,8},{8,0},{16,24},{24,16},{32,40},{40,32},{48,56},{56,48},{64,72... | collective-permute-start | bytes 1671176 | tf_op jit(solution)/shard_map/ppermute | solution.py:110
  124.3 2.1 %collective-permute-done.10 = f32[2,2,2,2,2,17,256]{6,4,5,3,2,1,0:T(2,128)S(1)} collective-permute-done((f32[2,2,2,2,2,17,256]{6,4,5,3,2,1,0:T(2,128)}, f32[2,2,2,2,2,17,256]{6,4,5,3,2,1,0:T(2,128)S(1)}, u32[]{:S(2)}, u32[]{:S(2)}) %collective-permute-start.10) | collective-permute-done | bytes 557088 | tf_op jit(solution)/shard_map/ppermute | solution.py:110
  126.4 0.5 bitcast_add_fusion
  127.0 3.6 %collective-permute-start.11 = (f32[2,2,2,2,17,256]{5,3,4,2,1,0:T(2,128)S(1)}, f32[2,2,2,2,17,256]{5,3,4,2,1,0:T(2,128)S(1)}, u32[]{:S(2)}, u32[]{:S(2)}) collective-permute-start(f32[2,2,2,2,17,256]{5,3,4,2,1,0:T(2,128)S(1)} %select_bitcast_fusion.1), channel_id=1, source_target_pairs={{0,16},{8,24},{16,0},{24,8},{32,48},{40,56},{48,32},{56,40},{64,80... | collective-permute-start | bytes 835592 | tf_op jit(solution)/shard_map/ppermute | solution.py:110
  130.6 7.0 %collective-permute-done.11 = f32[2,2,2,2,17,256]{5,3,4,2,1,0:T(2,128)S(1)} collective-permute-done((f32[2,2,2,2,17,256]{5,3,4,2,1,0:T(2,128)S(1)}, f32[2,2,2,2,17,256]{5,3,4,2,1,0:T(2,128)S(1)}, u32[]{:S(2)}, u32[]{:S(2)}) %collective-permute-start.11) | collective-permute-done | bytes 278560 | tf_op jit(solution)/shard_map/ppermute | solution.py:110
  138.1 4.6 %collective-permute-start.12 = (f32[2,2,2,17,256]{4,2,3,1,0:T(2,128)S(1)}, f32[2,2,2,17,256]{4,2,3,1,0:T(2,128)S(1)}, u32[]{:S(2)}, u32[]{:S(2)}) collective-permute-start(f32[2,2,2,17,256]{4,2,3,1,0:T(2,128)S(1)} %bitcast.109), channel_id=1, source_target_pairs={{0,32},{8,40},{16,48},{24,56},{32,0},{40,8},{48,16},{56,24},{64,96... | collective-permute-start | bytes 417800 | tf_op jit(solution)/shard_map/ppermute | solution.py:110
  142.8 6.1 %collective-permute-done.12 = f32[2,2,2,17,256]{4,2,3,1,0:T(2,128)S(1)} collective-permute-done((f32[2,2,2,17,256]{4,2,3,1,0:T(2,128)S(1)}, f32[2,2,2,17,256]{4,2,3,1,0:T(2,128)S(1)}, u32[]{:S(2)}, u32[]{:S(2)}) %collective-permute-start.12) | collective-permute-done | bytes 139296 | tf_op jit(solution)/shard_map/ppermute | solution.py:110
  149.1 7.9 %collective-permute-start.13 = (f32[2,2,17,256]{3,1,2,0:T(2,128)S(1)}, f32[2,2,17,256]{3,1,2,0:T(2,128)S(1)}, u32[]{:S(2)}, u32[]{:S(2)}) collective-permute-start(f32[2,2,17,256]{3,1,2,0:T(2,128)S(1)} %bitcast.110), channel_id=1, source_target_pairs={{0,64},{8,72},{16,80},{24,88},{32,96},{40,104},{48,112},{56,120},{... | collective-permute-start | bytes 208904 | tf_op jit(solution)/shard_map/ppermute | solution.py:110
  157.0 2.3 %collective-permute-done.13 = f32[2,2,17,256]{3,1,2,0:T(2,128)S(1)} collective-permute-done((f32[2,2,17,256]{3,1,2,0:T(2,128)S(1)}, f32[2,2,17,256]{3,1,2,0:T(2,128)S(1)}, u32[]{:S(2)}, u32[]{:S(2)}) %collective-permute-start.13) | collective-permute-done | bytes 69664 | tf_op jit(solution)/shard_map/ppermute | solution.py:110
  159.5 4.0 %collective-permute-start.14 = (f32[2,17,256]{2,0,1:T(2,128)S(1)}, f32[2,17,256]{2,0,1:T(2,128)S(1)}, u32[]{:S(2)}, u32[]{:S(2)}) collective-permute-start(f32[2,17,256]{2,0,1:T(2,128)S(1)} %bitcast.111), channel_id=1, source_target_pairs={{0,128},{8,136},{16,144},{24,152},{32,160},{40,168},{48,176},{56,1... | collective-permute-start | bytes 104456 | tf_op jit(solution)/shard_map/ppermute | solution.py:110
  163.5 1.9 %collective-permute-done.14 = f32[2,17,256]{2,0,1:T(2,128)S(1)} collective-permute-done((f32[2,17,256]{2,0,1:T(2,128)S(1)}, f32[2,17,256]{2,0,1:T(2,128)S(1)}, u32[]{:S(2)}, u32[]{:S(2)}) %collective-permute-start.14) | collective-permute-done | bytes 34848 | tf_op jit(solution)/shard_map/ppermute | solution.py:110
  165.5 3.9 %collective-permute-start.15 = (f32[17,256]{1,0:T(8,128)S(1)}, f32[17,256]{1,0:T(8,128)S(1)}, u32[]{:S(2)}, u32[]{:S(2)}) collective-permute-start(f32[17,256]{1,0:T(8,128)S(1)} %bitcast.112), channel_id=1, source_target_pairs={{0,256},{8,264},{16,272},{24,280},{32,288},{40,296},{48,304},{56,3... | collective-permute-start | bytes 52232 | tf_op jit(solution)/shard_map/ppermute | solution.py:110
  169.4 3.3 %collective-permute-done.15 = f32[17,256]{1,0:T(8,128)S(1)} collective-permute-done((f32[17,256]{1,0:T(8,128)S(1)}, f32[17,256]{1,0:T(8,128)S(1)}, u32[]{:S(2)}, u32[]{:S(2)}) %collective-permute-start.15) | collective-permute-done | bytes 17440 | tf_op jit(solution)/shard_map/ppermute | solution.py:110
  172.8 0.9 broadcast_multiply_fusion
  173.6 0.7 fusion.116
  (55 shorter events, 4.2 us)
Async XLA Ops:
  7.2 105.6 %all-gather.2.cloned.1.call-start = ((), (), s32[]{:S(2)}) async-start(), calls=%async_computation | async-start | bytes 2359296 | tf_op jit(solution)/shard_map/all_gather | solution.py:128
  8.3 15.8 %collective-permute-start = (bf16[4,16,16,128]{3,2,1,0:T(8,128)(2,1)S(1)}, bf16[4,16,16,128]{3,2,1,0:T(8,128)(2,1)S(1)}, u32[]{:S(2)}, u32[]{:S(2)}) collective-permute-start(bf16[4,16,16,128]{3,2,1,0:T(8,128)(2,1)S(1)} %convert_element_type.233), channel_id=1, source_target_pairs={{8,0},{16,8},{24,16},{32,24},{40,32},{48,40},{56,48},{64,56},{72,6... | collective-permute-start | bytes 786440 | tf_op jit(solution)/shard_map/ppermute | solution.py:22
  18.7 9.8 %collective-permute-start.1 = (bf16[4,16,16,128]{3,2,1,0:T(8,128)(2,1)S(1)}, bf16[4,16,16,128]{3,2,1,0:T(8,128)(2,1)S(1)}, u32[]{:S(2)}, u32[]{:S(2)}) collective-permute-start(bf16[4,16,16,128]{3,2,1,0:T(8,128)(2,1)S(1)} %convert_element_type.233), channel_id=1, source_target_pairs={{0,8},{8,16},{16,24},{24,32},{32,40},{40,48},{48,56},{56,64},{64,7... | collective-permute-start | bytes 786440 | tf_op jit(solution)/shard_map/ppermute | solution.py:21
  21.4 7.1 %copy-start = (f32[4,16,16,128]{3,2,1,0:T(8,128)S(1)}, f32[4,16,16,128]{3,2,1,0:T(8,128)}, u32[]{:S(2)}) copy-start(f32[4,16,16,128]{3,2,1,0:T(8,128)} %param.2) | copy-start | bytes 1572868
  21.4 7.2 %copy-start.2 = (f32[4,16,16]{2,1,0:T(8,128)S(1)}, f32[4,16,16]{2,1,0:T(8,128)}, u32[]{:S(2)}) copy-start(f32[4,16,16]{2,1,0:T(8,128)} %param.3) | copy-start | bytes 12292
  28.9 6.5 %collective-permute-start.2 = (bf16[4,16,16,128]{3,2,1,0:T(8,128)(2,1)S(1)}, bf16[4,16,16,128]{3,2,1,0:T(8,128)(2,1)S(1)}, u32[]{:S(2)}, u32[]{:S(2)}) collective-permute-start(bf16[4,16,16,128]{3,2,1,0:T(8,128)(2,1)S(1)} %get-tuple-element.9), channel_id=1, source_target_pairs={{8,0},{16,8},{24,16},{32,24},{40,32},{48,40},{56,48},{64,56},{72,6... | collective-permute-start | bytes 786440 | tf_op jit(solution)/shard_map/ppermute | solution.py:22
  30.8 9.8 %collective-permute-start.3 = (bf16[4,16,16,128]{3,2,1,0:T(8,128)(2,1)S(1)}, bf16[4,16,16,128]{3,2,1,0:T(8,128)(2,1)S(1)}, u32[]{:S(2)}, u32[]{:S(2)}) collective-permute-start(bf16[4,16,16,128]{3,2,1,0:T(8,128)(2,1)S(1)} %get-tuple-element.9), channel_id=1, source_target_pairs={{0,8},{8,16},{16,24},{24,32},{32,40},{40,48},{48,56},{56,64},{64,7... | collective-permute-start | bytes 786440 | tf_op jit(solution)/shard_map/ppermute | solution.py:21
  41.1 6.5 %collective-permute-start.4 = (bf16[4,16,16,128]{3,2,1,0:T(8,128)(2,1)S(1)}, bf16[4,16,16,128]{3,2,1,0:T(8,128)(2,1)S(1)}, u32[]{:S(2)}, u32[]{:S(2)}) collective-permute-start(bf16[4,16,16,128]{3,2,1,0:T(8,128)(2,1)S(1)} %get-tuple-element.7), channel_id=1, source_target_pairs={{8,0},{16,8},{24,16},{32,24},{40,32},{48,40},{56,48},{64,56},{72,6... | collective-permute-start | bytes 786440 | tf_op jit(solution)/shard_map/ppermute | solution.py:22
  43.1 9.8 %collective-permute-start.5 = (bf16[4,16,16,128]{3,2,1,0:T(8,128)(2,1)S(1)}, bf16[4,16,16,128]{3,2,1,0:T(8,128)(2,1)S(1)}, u32[]{:S(2)}, u32[]{:S(2)}) collective-permute-start(bf16[4,16,16,128]{3,2,1,0:T(8,128)(2,1)S(1)} %get-tuple-element.7), channel_id=1, source_target_pairs={{0,8},{8,16},{16,24},{24,32},{32,40},{40,48},{48,56},{56,64},{64,7... | collective-permute-start | bytes 786440 | tf_op jit(solution)/shard_map/ppermute | solution.py:21
  53.3 6.5 %collective-permute-start.6 = (bf16[4,16,16,128]{3,2,1,0:T(8,128)(2,1)S(1)}, bf16[4,16,16,128]{3,2,1,0:T(8,128)(2,1)S(1)}, u32[]{:S(2)}, u32[]{:S(2)}) collective-permute-start(bf16[4,16,16,128]{3,2,1,0:T(8,128)(2,1)S(1)} %get-tuple-element.5), channel_id=1, source_target_pairs={{8,0},{16,8},{24,16},{32,24},{40,32},{48,40},{56,48},{64,56},{72,6... | collective-permute-start | bytes 786440 | tf_op jit(solution)/shard_map/ppermute | solution.py:22
  55.2 9.8 %collective-permute-start.7 = (bf16[4,16,16,128]{3,2,1,0:T(8,128)(2,1)S(1)}, bf16[4,16,16,128]{3,2,1,0:T(8,128)(2,1)S(1)}, u32[]{:S(2)}, u32[]{:S(2)}) collective-permute-start(bf16[4,16,16,128]{3,2,1,0:T(8,128)(2,1)S(1)} %get-tuple-element.5), channel_id=1, source_target_pairs={{0,8},{8,16},{16,24},{24,32},{32,40},{40,48},{48,56},{56,64},{64,7... | collective-permute-start | bytes 786440 | tf_op jit(solution)/shard_map/ppermute | solution.py:21
  66.4 10.1 %collective-permute-start.9 = (bf16[4,16,16,128]{3,2,1,0:T(8,128)(2,1)}, bf16[4,16,16,128]{3,2,1,0:T(8,128)(2,1)S(1)}, u32[]{:S(2)}, u32[]{:S(2)}) collective-permute-start(bf16[4,16,16,128]{3,2,1,0:T(8,128)(2,1)} %convert_element_type.261), channel_id=1, source_target_pairs={{0,8},{8,16},{16,24},{24,32},{32,40},{40,48},{48,56},{56,64},{64,7... | collective-permute-start | bytes 786440 | tf_op jit(solution)/shard_map/ppermute | solution.py:21
  68.3 9.9 %collective-permute-start.8 = (bf16[4,16,16,128]{3,2,1,0:T(8,128)(2,1)}, bf16[4,16,16,128]{3,2,1,0:T(8,128)(2,1)S(1)}, u32[]{:S(2)}, u32[]{:S(2)}) collective-permute-start(bf16[4,16,16,128]{3,2,1,0:T(8,128)(2,1)} %convert_element_type.261), channel_id=1, source_target_pairs={{8,0},{16,8},{24,16},{32,24},{40,32},{48,40},{56,48},{64,56},{72,6... | collective-permute-start | bytes 786440 | tf_op jit(solution)/shard_map/ppermute | solution.py:22
  115.0 2.9 %copy-start.1 = (bf16[4,16,16,128]{3,2,1,0:T(8,128)(2,1)S(1)}, bf16[4,16,16,128]{3,2,1,0:T(8,128)(2,1)}, u32[]{:S(2)}) copy-start(bf16[4,16,16,128]{3,2,1,0:T(8,128)(2,1)} %convert_element_type.261) | copy-start | bytes 786436
  122.4 4.0 %collective-permute-start.10 = (f32[2,2,2,2,2,17,256]{6,4,5,3,2,1,0:T(2,128)}, f32[2,2,2,2,2,17,256]{6,4,5,3,2,1,0:T(2,128)S(1)}, u32[]{:S(2)}, u32[]{:S(2)}) collective-permute-start(f32[2,2,2,2,2,17,256]{6,4,5,3,2,1,0:T(2,128)} %copy.196), channel_id=1, source_target_pairs={{0,8},{8,0},{16,24},{24,16},{32,40},{40,32},{48,56},{56,48},{64,72... | collective-permute-start | bytes 1671176 | tf_op jit(solution)/shard_map/ppermute | solution.py:110
  127.0 10.6 %collective-permute-start.11 = (f32[2,2,2,2,17,256]{5,3,4,2,1,0:T(2,128)S(1)}, f32[2,2,2,2,17,256]{5,3,4,2,1,0:T(2,128)S(1)}, u32[]{:S(2)}, u32[]{:S(2)}) collective-permute-start(f32[2,2,2,2,17,256]{5,3,4,2,1,0:T(2,128)S(1)} %select_bitcast_fusion.1), channel_id=1, source_target_pairs={{0,16},{8,24},{16,0},{24,8},{32,48},{40,56},{48,32},{56,40},{64,80... | collective-permute-start | bytes 835592 | tf_op jit(solution)/shard_map/ppermute | solution.py:110
  138.1 10.7 %collective-permute-start.12 = (f32[2,2,2,17,256]{4,2,3,1,0:T(2,128)S(1)}, f32[2,2,2,17,256]{4,2,3,1,0:T(2,128)S(1)}, u32[]{:S(2)}, u32[]{:S(2)}) collective-permute-start(f32[2,2,2,17,256]{4,2,3,1,0:T(2,128)S(1)} %bitcast.109), channel_id=1, source_target_pairs={{0,32},{8,40},{16,48},{24,56},{32,0},{40,8},{48,16},{56,24},{64,96... | collective-permute-start | bytes 417800 | tf_op jit(solution)/shard_map/ppermute | solution.py:110
  149.1 10.2 %collective-permute-start.13 = (f32[2,2,17,256]{3,1,2,0:T(2,128)S(1)}, f32[2,2,17,256]{3,1,2,0:T(2,128)S(1)}, u32[]{:S(2)}, u32[]{:S(2)}) collective-permute-start(f32[2,2,17,256]{3,1,2,0:T(2,128)S(1)} %bitcast.110), channel_id=1, source_target_pairs={{0,64},{8,72},{16,80},{24,88},{32,96},{40,104},{48,112},{56,120},{... | collective-permute-start | bytes 208904 | tf_op jit(solution)/shard_map/ppermute | solution.py:110
  159.5 5.9 %collective-permute-start.14 = (f32[2,17,256]{2,0,1:T(2,128)S(1)}, f32[2,17,256]{2,0,1:T(2,128)S(1)}, u32[]{:S(2)}, u32[]{:S(2)}) collective-permute-start(f32[2,17,256]{2,0,1:T(2,128)S(1)} %bitcast.111), channel_id=1, source_target_pairs={{0,128},{8,136},{16,144},{24,152},{32,160},{40,168},{48,176},{56,1... | collective-permute-start | bytes 104456 | tf_op jit(solution)/shard_map/ppermute | solution.py:110
  165.5 7.2 %collective-permute-start.15 = (f32[17,256]{1,0:T(8,128)S(1)}, f32[17,256]{1,0:T(8,128)S(1)}, u32[]{:S(2)}, u32[]{:S(2)}) collective-permute-start(f32[17,256]{1,0:T(8,128)S(1)} %bitcast.112), channel_id=1, source_target_pairs={{0,256},{8,264},{16,272},{24,280},{32,288},{40,296},{48,304},{56,3... | collective-permute-start | bytes 52232 | tf_op jit(solution)/shard_map/ppermute | solution.py:110
Sparse Core Ops, SparseCore 0:
  66.4 46.3 all-gather.1
where the time goes:
time: 182 us; the launch traced here: 181 us
  waiting for transfers between devices  78.5 us (43%)
  starting transfers between devices  59.1 us (32%)
  between operations  14.6 us (8%)
  matrix products  11.8 us (6%)
  other arithmetic  11 us (6%)
  local copies, waits for them, and re-layouts  6.16 us (3%)
    all_gather x1, waiting for transfers between devices, on_device(): orbitals_all = lax.all_gather(rounded_orbitals, 'orb', axis=1, tiled=True)  34.1 us
    ppermute x6, starting transfers between devices, reduce_scatter_grid(): buf = keep + lax.ppermute(send, 'grid', pairs)  25.9 us
    ppermute x6, waiting for transfers between devices, reduce_scatter_grid(): buf = keep + lax.ppermute(send, 'grid', pairs)  22.7 us
    ppermute x5, starting transfers between devices, halo_layers(): after = lax.ppermute(initial, 'grid', down).astype(shard.dtype)  22.1 us
    ppermute x5, waiting for transfers between devices, halo_layers(): before = lax.ppermute(last, 'grid', up).astype(shard.dtype)  19.8 us
    ppermute x5, starting transfers between devices, halo_layers(): before = lax.ppermute(last, 'grid', up).astype(shard.dtype)  11 us
    dot_general x5, matrix products, apply_hamiltonian(): jnp.einsum('pq,zqo->zpo', plane, flat, precision=lax.Precision.HIGHEST, p...  10.4 us
  transfers between devices with their start and end apart: 17, of which 12 were waited for; matrix products, arithmetic and copies ran while one was open for 7% of the time, Pallas kernels for 0%

commit v1 on v0

--- a/solution.py
+++ b/solution.py
@@ -125,7 +125,9 @@
         .astype(jnp.bfloat16)
         .reshape(point_count, own_width)
     )
-    orbitals_all = lax.all_gather(rounded_orbitals, "orb", axis=1, tiled=True)
+    orbitals_all = jnp.concatenate(
+        lax.all_to_all(jnp.stack([rounded_orbitals] * lax.axis_size("orb")), "orb", 0, 0), axis=1
+    )
     total_width = orbitals_all.shape[1]
     rows = total_width // grid_size
     hamiltonian_part = contract_points(orbitals_all, rounded_image)

time: 182 us -> 173 us (0.951)
  the two profiles are of different devices: /device:TPU:2 before, /device:TPU:6 now
where the time goes in v1:
time: 173 us; the launch traced here: 172 us
  waiting for transfers between devices  87.5 us (51%)
  starting transfers between devices  53.6 us (31%)
  matrix products  12.6 us (7%)
  other arithmetic  11.4 us (7%)
  local copies, waits for them, and re-layouts  6.04 us (3%)
    ppermute x6, waiting for transfers between devices, reduce_scatter_grid(): buf = keep + lax.ppermute(send, 'grid', pairs)  35.4 us
    all_to_all x1, waiting for transfers between devices, on_device(): lax.all_to_all(jnp.stack([rounded_orbitals] * lax.axis_size('orb')), 'orb...  32.3 us
    ppermute x5, starting transfers between devices, halo_layers(): after = lax.ppermute(initial, 'grid', down).astype(shard.dtype)  22.3 us
    ppermute x5, waiting for transfers between devices, halo_layers(): before = lax.ppermute(last, 'grid', up).astype(shard.dtype)  19.8 us
    ppermute x6, starting transfers between devices, reduce_scatter_grid(): buf = keep + lax.ppermute(send, 'grid', pairs)  13.1 us
    dot_general x5, matrix products, apply_hamiltonian(): jnp.einsum('pq,zqo->zpo', plane, flat, precision=lax.Precision.HIGHEST, p...  11.2 us
    ppermute x5, starting transfers between devices, halo_layers(): before = lax.ppermute(last, 'grid', up).astype(shard.dtype)  11 us
    all_to_all x1, starting transfers between devices, on_device(): lax.all_to_all(jnp.stack([rounded_orbitals] * lax.axis_size('orb')), 'orb...  7.1 us
  transfers between devices with their start and end apart: 17, of which 11 were waited for; matrix products, arithmetic and copies ran while one was open for 10% of the time, Pallas kernels for 0%

profile of v1, /device:TPU:6, one launch (start us, length us, event | category | flops | bytes accessed | tf_op | source)
XLA Modules:
  0.0 172.3 jit_solution(246250090848900902)
XLA Ops:
  0.6 1.1 convert_element_type.234
  1.7 10.7 %collective-permute-start = (bf16[4,16,16,128]{3,2,1,0:T(8,128)(2,1)S(1)}, bf16[4,16,16,128]{3,2,1,0:T(8,128)(2,1)S(1)}, u32[]{:S(2)}, u32[]{:S(2)}) collective-permute-start(bf16[4,16,16,128]{3,2,1,0:T(8,128)(2,1)S(1)} %convert_element_type.234), channel_id=1, source_target_pairs={{8,0},{16,8},{24,16},{32,24},{40,32},{48,40},{56,48},{64,56},{72,6... | collective-permute-start | bytes 786440 | tf_op jit(solution)/shard_map/ppermute | solution.py:22
  12.4 1.9 %collective-permute-start.1 = (bf16[4,16,16,128]{3,2,1,0:T(8,128)(2,1)S(1)}, bf16[4,16,16,128]{3,2,1,0:T(8,128)(2,1)S(1)}, u32[]{:S(2)}, u32[]{:S(2)}) collective-permute-start(bf16[4,16,16,128]{3,2,1,0:T(8,128)(2,1)S(1)} %convert_element_type.234), channel_id=1, source_target_pairs={{0,8},{8,16},{16,24},{24,32},{32,40},{40,48},{48,56},{56,64},{64,7... | collective-permute-start | bytes 786440 | tf_op jit(solution)/shard_map/ppermute | solution.py:21
  14.3 0.8 broadcast_multiply_fusion.2
  15.1 2.7 %fusion.102 = f32[256,4,128]{2,0,1:T(8,128)S(1)} fusion(f32[4,256,128]{2,1,0:T(8,128)} %bitcast.101, s32[256]{0:T(256)S(1)} %get-tuple-element.22, s32[256]{0:T(256)S(1)} %get-tuple-element.23), kind=kOutput, calls=%fused_computation.176 | convolution fusion | flops 408944640 | bytes 1050624 | tf_op jit(solution)/shard_map/pq,zqo->zpo/dot_general | solution.py:57
  17.9 4.3 %collective-permute-done.1 = bf16[4,16,16,128]{3,2,1,0:T(8,128)(2,1)S(1)} collective-permute-done((bf16[4,16,16,128]{3,2,1,0:T(8,128)(2,1)S(1)}, bf16[4,16,16,128]{3,2,1,0:T(8,128)(2,1)S(1)}, u32[]{:S(2)}, u32[]{:S(2)}) %collective-permute-start.1) | collective-permute-done | bytes 262176 | tf_op jit(solution)/shard_map/ppermute | solution.py:21
  22.6 1.9 %collective-permute-start.2 = (bf16[4,16,16,128]{3,2,1,0:T(8,128)(2,1)S(1)}, bf16[4,16,16,128]{3,2,1,0:T(8,128)(2,1)S(1)}, u32[]{:S(2)}, u32[]{:S(2)}) collective-permute-start(bf16[4,16,16,128]{3,2,1,0:T(8,128)(2,1)S(1)} %get-tuple-element.9), channel_id=1, source_target_pairs={{8,0},{16,8},{24,16},{32,24},{40,32},{48,40},{56,48},{64,56},{72,6... | collective-permute-start | bytes 786440 | tf_op jit(solution)/shard_map/ppermute | solution.py:22
  24.6 2.4 %collective-permute-start.3 = (bf16[4,16,16,128]{3,2,1,0:T(8,128)(2,1)S(1)}, bf16[4,16,16,128]{3,2,1,0:T(8,128)(2,1)S(1)}, u32[]{:S(2)}, u32[]{:S(2)}) collective-permute-start(bf16[4,16,16,128]{3,2,1,0:T(8,128)(2,1)S(1)} %get-tuple-element.9), channel_id=1, source_target_pairs={{0,8},{8,16},{16,24},{24,32},{32,40},{40,48},{48,56},{56,64},{64,7... | collective-permute-start | bytes 786440 | tf_op jit(solution)/shard_map/ppermute | solution.py:21
  27.0 1.9 %convolution_bitcast_fusion.3 = f32[4,256,128]{1,2,0:T(8,128)S(1)} fusion(f32[4,256,128]{2,1,0:T(8,128)S(1)} %bitcast.106, s32[256]{0:T(256)S(1)} %get-tuple-element.22, s32[256]{0:T(256)S(1)} %get-tuple-element.23), kind=kOutput, calls=%fused_computation.44 | convolution fusion | flops 408944640 | bytes 1050624 | tf_op jit(solution)/shard_map/pq,zqo->zpo/dot_general | solution.py:57
  29.2 5.1 %collective-permute-done.3 = bf16[4,16,16,128]{3,2,1,0:T(8,128)(2,1)S(1)} collective-permute-done((bf16[4,16,16,128]{3,2,1,0:T(8,128)(2,1)S(1)}, bf16[4,16,16,128]{3,2,1,0:T(8,128)(2,1)S(1)}, u32[]{:S(2)}, u32[]{:S(2)}) %collective-permute-start.3) | collective-permute-done | bytes 262176 | tf_op jit(solution)/shard_map/ppermute | solution.py:21
  34.8 1.9 %collective-permute-start.4 = (bf16[4,16,16,128]{3,2,1,0:T(8,128)(2,1)S(1)}, bf16[4,16,16,128]{3,2,1,0:T(8,128)(2,1)S(1)}, u32[]{:S(2)}, u32[]{:S(2)}) collective-permute-start(bf16[4,16,16,128]{3,2,1,0:T(8,128)(2,1)S(1)} %get-tuple-element.7), channel_id=1, source_target_pairs={{8,0},{16,8},{24,16},{32,24},{40,32},{48,40},{56,48},{64,56},{72,6... | collective-permute-start | bytes 786440 | tf_op jit(solution)/shard_map/ppermute | solution.py:22
  36.8 2.4 %collective-permute-start.5 = (bf16[4,16,16,128]{3,2,1,0:T(8,128)(2,1)S(1)}, bf16[4,16,16,128]{3,2,1,0:T(8,128)(2,1)S(1)}, u32[]{:S(2)}, u32[]{:S(2)}) collective-permute-start(bf16[4,16,16,128]{3,2,1,0:T(8,128)(2,1)S(1)} %get-tuple-element.7), channel_id=1, source_target_pairs={{0,8},{8,16},{16,24},{24,32},{32,40},{40,48},{48,56},{56,64},{64,7... | collective-permute-start | bytes 786440 | tf_op jit(solution)/shard_map/ppermute | solution.py:21
  39.2 1.9 %convolution_bitcast_fusion.2 = f32[4,256,128]{1,2,0:T(8,128)S(1)} fusion(f32[4,256,128]{2,1,0:T(8,128)S(1)} %bitcast.102, s32[256]{0:T(256)S(1)} %get-tuple-element.22, s32[256]{0:T(256)S(1)} %get-tuple-element.23), kind=kOutput, calls=%fused_computation.43 | convolution fusion | flops 408944640 | bytes 1050624 | tf_op jit(solution)/shard_map/pq,zqo->zpo/dot_general | solution.py:57
  41.4 5.2 %collective-permute-done.5 = bf16[4,16,16,128]{3,2,1,0:T(8,128)(2,1)S(1)} collective-permute-done((bf16[4,16,16,128]{3,2,1,0:T(8,128)(2,1)S(1)}, bf16[4,16,16,128]{3,2,1,0:T(8,128)(2,1)S(1)}, u32[]{:S(2)}, u32[]{:S(2)}) %collective-permute-start.5) | collective-permute-done | bytes 262176 | tf_op jit(solution)/shard_map/ppermute | solution.py:21
  47.0 1.9 %collective-permute-start.6 = (bf16[4,16,16,128]{3,2,1,0:T(8,128)(2,1)S(1)}, bf16[4,16,16,128]{3,2,1,0:T(8,128)(2,1)S(1)}, u32[]{:S(2)}, u32[]{:S(2)}) collective-permute-start(bf16[4,16,16,128]{3,2,1,0:T(8,128)(2,1)S(1)} %get-tuple-element.5), channel_id=1, source_target_pairs={{8,0},{16,8},{24,16},{32,24},{40,32},{48,40},{56,48},{64,56},{72,6... | collective-permute-start | bytes 786440 | tf_op jit(solution)/shard_map/ppermute | solution.py:22
  49.0 2.4 %collective-permute-start.7 = (bf16[4,16,16,128]{3,2,1,0:T(8,128)(2,1)S(1)}, bf16[4,16,16,128]{3,2,1,0:T(8,128)(2,1)S(1)}, u32[]{:S(2)}, u32[]{:S(2)}) collective-permute-start(bf16[4,16,16,128]{3,2,1,0:T(8,128)(2,1)S(1)} %get-tuple-element.5), channel_id=1, source_target_pairs={{0,8},{8,16},{16,24},{24,32},{32,40},{40,48},{48,56},{56,64},{64,7... | collective-permute-start | bytes 786440 | tf_op jit(solution)/shard_map/ppermute | solution.py:21
  51.4 1.9 %convolution_bitcast_fusion.1 = f32[4,256,128]{1,2,0:T(8,128)S(1)} fusion(f32[4,256,128]{2,1,0:T(8,128)S(1)} %bitcast.111, s32[256]{0:T(256)S(1)} %get-tuple-element.22, s32[256]{0:T(256)S(1)} %get-tuple-element.23), kind=kOutput, calls=%fused_computation.42 | convolution fusion | flops 408944640 | bytes 1050624 | tf_op jit(solution)/shard_map/pq,zqo->zpo/dot_general | solution.py:57
  53.6 5.2 %collective-permute-done.7 = bf16[4,16,16,128]{3,2,1,0:T(8,128)(2,1)S(1)} collective-permute-done((bf16[4,16,16,128]{3,2,1,0:T(8,128)(2,1)S(1)}, bf16[4,16,16,128]{3,2,1,0:T(8,128)(2,1)S(1)}, u32[]{:S(2)}, u32[]{:S(2)}) %collective-permute-start.7) | collective-permute-done | bytes 262176 | tf_op jit(solution)/shard_map/ppermute | solution.py:21
  59.4 1.6 stack.3
  61.0 7.1 %all-to-all-start = ((bf16[8,1024,128]{1,2,0:T(8,128)(2,1)}), bf16[8,1024,128]{1,2,0:T(8,128)(2,1)S(1)}, u32[]{:S(2)}, u32[]{:S(2)}) async-start(bf16[8,1024,128]{1,2,0:T(8,128)(2,1)} %stack.3), calls=%async_computation | async-start | bytes 4194304 | tf_op jit(solution)/shard_map/all_to_all | solution.py:129
  68.2 1.9 %collective-permute-start.9 = (bf16[4,16,16,128]{3,2,1,0:T(8,128)(2,1)S(1)}, bf16[4,16,16,128]{3,2,1,0:T(8,128)(2,1)}, u32[]{:S(2)}, u32[]{:S(2)}) collective-permute-start(bf16[4,16,16,128]{3,2,1,0:T(8,128)(2,1)S(1)} %convert_element_type.262), channel_id=1, source_target_pairs={{0,8},{8,16},{16,24},{24,32},{32,40},{40,48},{48,56},{56,64},{64,7... | collective-permute-start | bytes 786440 | tf_op jit(solution)/shard_map/ppermute | solution.py:21
  70.1 5.9 %collective-permute-start.8 = (bf16[4,16,16,128]{3,2,1,0:T(8,128)(2,1)S(1)}, bf16[4,16,16,128]{3,2,1,0:T(8,128)(2,1)}, u32[]{:S(2)}, u32[]{:S(2)}) collective-permute-start(bf16[4,16,16,128]{3,2,1,0:T(8,128)(2,1)S(1)} %convert_element_type.262), channel_id=1, source_target_pairs={{8,0},{16,8},{24,16},{32,24},{40,32},{48,40},{56,48},{64,56},{72,6... | collective-permute-start | bytes 786440 | tf_op jit(solution)/shard_map/ppermute | solution.py:22
  76.1 2.7 %convolution_bitcast_fusion = f32[4,256,128]{1,2,0:T(8,128)} fusion(f32[4,256,128]{2,1,0:T(8,128)S(1)} %bitcast.100, s32[256]{0:T(256)S(1)} %get-tuple-element.22, s32[256]{0:T(256)S(1)} %get-tuple-element.23), kind=kOutput, calls=%fused_computation.41 | convolution fusion | flops 408944640 | bytes 1050624 | tf_op jit(solution)/shard_map/pq,zqo->zpo/dot_general | solution.py:57
  78.8 1.2 copy.193
  80.1 1.0 convert_element_type.264
  81.1 1.0 convert_element_type.263
  82.1 1.0 fusion.9
  83.2 32.3 %all-to-all-done = bf16[8,1024,128]{1,2,0:T(8,128)(2,1)S(1)} async-done(((bf16[8,1024,128]{1,2,0:T(8,128)(2,1)}), bf16[8,1024,128]{1,2,0:T(8,128)(2,1)S(1)}, u32[]{:S(2)}, u32[]{:S(2)}) %all-to-all-start) | async-done | bytes 2097184 | tf_op jit(solution)/shard_map/all_to_all | solution.py:129
  115.4 0.5 multiply_reduce_fusion
  116.0 0.7 fusion.204
  116.8 0.7 fusion.203
  117.6 0.8 copy.195
  118.4 0.6 maximum_maximum_fusion
  119.3 1.3 copy.196
  120.5 1.9 %collective-permute-start.10 = (f32[2,2,2,2,2,17,256]{6,4,5,3,2,1,0:T(2,128)}, f32[2,2,2,2,2,17,256]{6,4,5,3,2,1,0:T(2,128)S(1)}, u32[]{:S(2)}, u32[]{:S(2)}) collective-permute-start(f32[2,2,2,2,2,17,256]{6,4,5,3,2,1,0:T(2,128)} %copy.196), channel_id=1, source_target_pairs={{0,8},{8,0},{16,24},{24,16},{32,40},{40,32},{48,56},{56,48},{64,72... | collective-permute-start | bytes 1671176 | tf_op jit(solution)/shard_map/ppermute | solution.py:110
  122.4 2.1 %collective-permute-done.10 = f32[2,2,2,2,2,17,256]{6,4,5,3,2,1,0:T(2,128)S(1)} collective-permute-done((f32[2,2,2,2,2,17,256]{6,4,5,3,2,1,0:T(2,128)}, f32[2,2,2,2,2,17,256]{6,4,5,3,2,1,0:T(2,128)S(1)}, u32[]{:S(2)}, u32[]{:S(2)}) %collective-permute-start.10) | collective-permute-done | bytes 557088 | tf_op jit(solution)/shard_map/ppermute | solution.py:110
  125.2 1.9 %collective-permute-start.11 = (f32[2,2,2,2,17,256]{5,3,4,2,1,0:T(2,128)S(1)}, f32[2,2,2,2,17,256]{5,3,4,2,1,0:T(2,128)S(1)}, u32[]{:S(2)}, u32[]{:S(2)}) collective-permute-start(f32[2,2,2,2,17,256]{5,3,4,2,1,0:T(2,128)S(1)} %select_bitcast_fusion.1), channel_id=1, source_target_pairs={{0,16},{8,24},{16,0},{24,8},{32,48},{40,56},{48,32},{56,40},{64,80... | collective-permute-start | bytes 835592 | tf_op jit(solution)/shard_map/ppermute | solution.py:110
  127.1 8.7 %collective-permute-done.11 = f32[2,2,2,2,17,256]{5,3,4,2,1,0:T(2,128)S(1)} collective-permute-done((f32[2,2,2,2,17,256]{5,3,4,2,1,0:T(2,128)S(1)}, f32[2,2,2,2,17,256]{5,3,4,2,1,0:T(2,128)S(1)}, u32[]{:S(2)}, u32[]{:S(2)}) %collective-permute-start.11) | collective-permute-done | bytes 278560 | tf_op jit(solution)/shard_map/ppermute | solution.py:110
  136.3 1.9 %collective-permute-start.12 = (f32[2,2,2,17,256]{4,2,3,1,0:T(2,128)S(1)}, f32[2,2,2,17,256]{4,2,3,1,0:T(2,128)S(1)}, u32[]{:S(2)}, u32[]{:S(2)}) collective-permute-start(f32[2,2,2,17,256]{4,2,3,1,0:T(2,128)S(1)} %bitcast.114), channel_id=1, source_target_pairs={{0,32},{8,40},{16,48},{24,56},{32,0},{40,8},{48,16},{56,24},{64,96... | collective-permute-start | bytes 417800 | tf_op jit(solution)/shard_map/ppermute | solution.py:110
  138.3 8.7 %collective-permute-done.12 = f32[2,2,2,17,256]{4,2,3,1,0:T(2,128)S(1)} collective-permute-done((f32[2,2,2,17,256]{4,2,3,1,0:T(2,128)S(1)}, f32[2,2,2,17,256]{4,2,3,1,0:T(2,128)S(1)}, u32[]{:S(2)}, u32[]{:S(2)}) %collective-permute-start.12) | collective-permute-done | bytes 139296 | tf_op jit(solution)/shard_map/ppermute | solution.py:110
  147.3 1.9 %collective-permute-start.13 = (f32[2,2,17,256]{3,1,2,0:T(2,128)S(1)}, f32[2,2,17,256]{3,1,2,0:T(2,128)S(1)}, u32[]{:S(2)}, u32[]{:S(2)}) collective-permute-start(f32[2,2,17,256]{3,1,2,0:T(2,128)S(1)} %bitcast.115), channel_id=1, source_target_pairs={{0,64},{8,72},{16,80},{24,88},{32,96},{40,104},{48,112},{56,120},{... | collective-permute-start | bytes 208904 | tf_op jit(solution)/shard_map/ppermute | solution.py:110
  149.2 8.2 %collective-permute-done.13 = f32[2,2,17,256]{3,1,2,0:T(2,128)S(1)} collective-permute-done((f32[2,2,17,256]{3,1,2,0:T(2,128)S(1)}, f32[2,2,17,256]{3,1,2,0:T(2,128)S(1)}, u32[]{:S(2)}, u32[]{:S(2)}) %collective-permute-start.13) | collective-permute-done | bytes 69664 | tf_op jit(solution)/shard_map/ppermute | solution.py:110
  157.5 2.4 %collective-permute-start.14 = (f32[2,17,256]{2,0,1:T(2,128)S(1)}, f32[2,17,256]{2,0,1:T(2,128)S(1)}, u32[]{:S(2)}, u32[]{:S(2)}) collective-permute-start(f32[2,17,256]{2,0,1:T(2,128)S(1)} %bitcast.116), channel_id=1, source_target_pairs={{0,128},{8,136},{16,144},{24,152},{32,160},{40,168},{48,176},{56,1... | collective-permute-start | bytes 104456 | tf_op jit(solution)/shard_map/ppermute | solution.py:110
  159.9 3.4 %collective-permute-done.14 = f32[2,17,256]{2,0,1:T(2,128)S(1)} collective-permute-done((f32[2,17,256]{2,0,1:T(2,128)S(1)}, f32[2,17,256]{2,0,1:T(2,128)S(1)}, u32[]{:S(2)}, u32[]{:S(2)}) %collective-permute-start.14) | collective-permute-done | bytes 34848 | tf_op jit(solution)/shard_map/ppermute | solution.py:110
  163.4 3.0 %collective-permute-start.15 = (f32[17,256]{1,0:T(8,128)S(1)}, f32[17,256]{1,0:T(8,128)S(1)}, u32[]{:S(2)}, u32[]{:S(2)}) collective-permute-start(f32[17,256]{1,0:T(8,128)S(1)} %bitcast.117), channel_id=1, source_target_pairs={{0,256},{8,264},{16,272},{24,280},{32,288},{40,296},{48,304},{56,3... | collective-permute-start | bytes 52232 | tf_op jit(solution)/shard_map/ppermute | solution.py:110
  166.4 4.2 %collective-permute-done.15 = f32[17,256]{1,0:T(8,128)S(1)} collective-permute-done((f32[17,256]{1,0:T(8,128)S(1)}, f32[17,256]{1,0:T(8,128)S(1)}, u32[]{:S(2)}, u32[]{:S(2)}) %collective-permute-start.15) | collective-permute-done | bytes 17440 | tf_op jit(solution)/shard_map/ppermute | solution.py:110
  170.8 0.8 broadcast_multiply_fusion
  171.6 0.7 fusion.116
  (55 shorter events, 5.1 us)
Async XLA Ops:
  1.7 16.1 %collective-permute-start = (bf16[4,16,16,128]{3,2,1,0:T(8,128)(2,1)S(1)}, bf16[4,16,16,128]{3,2,1,0:T(8,128)(2,1)S(1)}, u32[]{:S(2)}, u32[]{:S(2)}) collective-permute-start(bf16[4,16,16,128]{3,2,1,0:T(8,128)(2,1)S(1)} %convert_element_type.234), channel_id=1, source_target_pairs={{8,0},{16,8},{24,16},{32,24},{40,32},{48,40},{56,48},{64,56},{72,6... | collective-permute-start | bytes 786440 | tf_op jit(solution)/shard_map/ppermute | solution.py:22
  12.4 9.8 %collective-permute-start.1 = (bf16[4,16,16,128]{3,2,1,0:T(8,128)(2,1)S(1)}, bf16[4,16,16,128]{3,2,1,0:T(8,128)(2,1)S(1)}, u32[]{:S(2)}, u32[]{:S(2)}) collective-permute-start(bf16[4,16,16,128]{3,2,1,0:T(8,128)(2,1)S(1)} %convert_element_type.234), channel_id=1, source_target_pairs={{0,8},{8,16},{16,24},{24,32},{32,40},{40,48},{48,56},{56,64},{64,7... | collective-permute-start | bytes 786440 | tf_op jit(solution)/shard_map/ppermute | solution.py:21
  15.1 7.1 %copy-start = (f32[4,16,16,128]{3,2,1,0:T(8,128)S(1)}, f32[4,16,16,128]{3,2,1,0:T(8,128)}, u32[]{:S(2)}) copy-start(f32[4,16,16,128]{3,2,1,0:T(8,128)} %param.2) | copy-start | bytes 1572868
  15.1 7.1 %copy-start.2 = (f32[4,16,16]{2,1,0:T(8,128)S(1)}, f32[4,16,16]{2,1,0:T(8,128)}, u32[]{:S(2)}) copy-start(f32[4,16,16]{2,1,0:T(8,128)} %param.3) | copy-start | bytes 12292
  22.6 6.5 %collective-permute-start.2 = (bf16[4,16,16,128]{3,2,1,0:T(8,128)(2,1)S(1)}, bf16[4,16,16,128]{3,2,1,0:T(8,128)(2,1)S(1)}, u32[]{:S(2)}, u32[]{:S(2)}) collective-permute-start(bf16[4,16,16,128]{3,2,1,0:T(8,128)(2,1)S(1)} %get-tuple-element.9), channel_id=1, source_target_pairs={{8,0},{16,8},{24,16},{32,24},{40,32},{48,40},{56,48},{64,56},{72,6... | collective-permute-start | bytes 786440 | tf_op jit(solution)/shard_map/ppermute | solution.py:22
  24.6 9.8 %collective-permute-start.3 = (bf16[4,16,16,128]{3,2,1,0:T(8,128)(2,1)S(1)}, bf16[4,16,16,128]{3,2,1,0:T(8,128)(2,1)S(1)}, u32[]{:S(2)}, u32[]{:S(2)}) collective-permute-start(bf16[4,16,16,128]{3,2,1,0:T(8,128)(2,1)S(1)} %get-tuple-element.9), channel_id=1, source_target_pairs={{0,8},{8,16},{16,24},{24,32},{32,40},{40,48},{48,56},{56,64},{64,7... | collective-permute-start | bytes 786440 | tf_op jit(solution)/shard_map/ppermute | solution.py:21
  34.8 6.5 %collective-permute-start.4 = (bf16[4,16,16,128]{3,2,1,0:T(8,128)(2,1)S(1)}, bf16[4,16,16,128]{3,2,1,0:T(8,128)(2,1)S(1)}, u32[]{:S(2)}, u32[]{:S(2)}) collective-permute-start(bf16[4,16,16,128]{3,2,1,0:T(8,128)(2,1)S(1)} %get-tuple-element.7), channel_id=1, source_target_pairs={{8,0},{16,8},{24,16},{32,24},{40,32},{48,40},{56,48},{64,56},{72,6... | collective-permute-start | bytes 786440 | tf_op jit(solution)/shard_map/ppermute | solution.py:22
  36.8 9.8 %collective-permute-start.5 = (bf16[4,16,16,128]{3,2,1,0:T(8,128)(2,1)S(1)}, bf16[4,16,16,128]{3,2,1,0:T(8,128)(2,1)S(1)}, u32[]{:S(2)}, u32[]{:S(2)}) collective-permute-start(bf16[4,16,16,128]{3,2,1,0:T(8,128)(2,1)S(1)} %get-tuple-element.7), channel_id=1, source_target_pairs={{0,8},{8,16},{16,24},{24,32},{32,40},{40,48},{48,56},{56,64},{64,7... | collective-permute-start | bytes 786440 | tf_op jit(solution)/shard_map/ppermute | solution.py:21
  47.0 6.5 %collective-permute-start.6 = (bf16[4,16,16,128]{3,2,1,0:T(8,128)(2,1)S(1)}, bf16[4,16,16,128]{3,2,1,0:T(8,128)(2,1)S(1)}, u32[]{:S(2)}, u32[]{:S(2)}) collective-permute-start(bf16[4,16,16,128]{3,2,1,0:T(8,128)(2,1)S(1)} %get-tuple-element.5), channel_id=1, source_target_pairs={{8,0},{16,8},{24,16},{32,24},{40,32},{48,40},{56,48},{64,56},{72,6... | collective-permute-start | bytes 786440 | tf_op jit(solution)/shard_map/ppermute | solution.py:22
  49.0 9.8 %collective-permute-start.7 = (bf16[4,16,16,128]{3,2,1,0:T(8,128)(2,1)S(1)}, bf16[4,16,16,128]{3,2,1,0:T(8,128)(2,1)S(1)}, u32[]{:S(2)}, u32[]{:S(2)}) collective-permute-start(bf16[4,16,16,128]{3,2,1,0:T(8,128)(2,1)S(1)} %get-tuple-element.5), channel_id=1, source_target_pairs={{0,8},{8,16},{16,24},{24,32},{32,40},{40,48},{48,56},{56,64},{64,7... | collective-permute-start | bytes 786440 | tf_op jit(solution)/shard_map/ppermute | solution.py:21
  61.0 54.4 %all-to-all-start = ((bf16[8,1024,128]{1,2,0:T(8,128)(2,1)}), bf16[8,1024,128]{1,2,0:T(8,128)(2,1)S(1)}, u32[]{:S(2)}, u32[]{:S(2)}) async-start(bf16[8,1024,128]{1,2,0:T(8,128)(2,1)} %stack.3), calls=%async_computation | async-start | bytes 4194304 | tf_op jit(solution)/shard_map/all_to_all | solution.py:129
  68.2 11.9 %collective-permute-start.9 = (bf16[4,16,16,128]{3,2,1,0:T(8,128)(2,1)S(1)}, bf16[4,16,16,128]{3,2,1,0:T(8,128)(2,1)}, u32[]{:S(2)}, u32[]{:S(2)}) collective-permute-start(bf16[4,16,16,128]{3,2,1,0:T(8,128)(2,1)S(1)} %convert_element_type.262), channel_id=1, source_target_pairs={{0,8},{8,16},{16,24},{24,32},{32,40},{40,48},{48,56},{56,64},{64,7... | collective-permute-start | bytes 786440 | tf_op jit(solution)/shard_map/ppermute | solution.py:21
  70.1 11.0 %collective-permute-start.8 = (bf16[4,16,16,128]{3,2,1,0:T(8,128)(2,1)S(1)}, bf16[4,16,16,128]{3,2,1,0:T(8,128)(2,1)}, u32[]{:S(2)}, u32[]{:S(2)}) collective-permute-start(bf16[4,16,16,128]{3,2,1,0:T(8,128)(2,1)S(1)} %convert_element_type.262), channel_id=1, source_target_pairs={{8,0},{16,8},{24,16},{32,24},{40,32},{48,40},{56,48},{64,56},{72,6... | collective-permute-start | bytes 786440 | tf_op jit(solution)/shard_map/ppermute | solution.py:22
  83.2 33.6 %copy-start.1 = (bf16[4,16,16,128]{3,2,1,0:T(8,128)(2,1)S(1)}, bf16[4,16,16,128]{3,2,1,0:T(8,128)(2,1)}, u32[]{:S(2)}) copy-start(bf16[4,16,16,128]{3,2,1,0:T(8,128)(2,1)} %fusion.9) | copy-start | bytes 786436
  120.5 4.0 %collective-permute-start.10 = (f32[2,2,2,2,2,17,256]{6,4,5,3,2,1,0:T(2,128)}, f32[2,2,2,2,2,17,256]{6,4,5,3,2,1,0:T(2,128)S(1)}, u32[]{:S(2)}, u32[]{:S(2)}) collective-permute-start(f32[2,2,2,2,2,17,256]{6,4,5,3,2,1,0:T(2,128)} %copy.196), channel_id=1, source_target_pairs={{0,8},{8,0},{16,24},{24,16},{32,40},{40,32},{48,56},{56,48},{64,72... | collective-permute-start | bytes 1671176 | tf_op jit(solution)/shard_map/ppermute | solution.py:110
  125.2 10.6 %collective-permute-start.11 = (f32[2,2,2,2,17,256]{5,3,4,2,1,0:T(2,128)S(1)}, f32[2,2,2,2,17,256]{5,3,4,2,1,0:T(2,128)S(1)}, u32[]{:S(2)}, u32[]{:S(2)}) collective-permute-start(f32[2,2,2,2,17,256]{5,3,4,2,1,0:T(2,128)S(1)} %select_bitcast_fusion.1), channel_id=1, source_target_pairs={{0,16},{8,24},{16,0},{24,8},{32,48},{40,56},{48,32},{56,40},{64,80... | collective-permute-start | bytes 835592 | tf_op jit(solution)/shard_map/ppermute | solution.py:110
  136.3 10.7 %collective-permute-start.12 = (f32[2,2,2,17,256]{4,2,3,1,0:T(2,128)S(1)}, f32[2,2,2,17,256]{4,2,3,1,0:T(2,128)S(1)}, u32[]{:S(2)}, u32[]{:S(2)}) collective-permute-start(f32[2,2,2,17,256]{4,2,3,1,0:T(2,128)S(1)} %bitcast.114), channel_id=1, source_target_pairs={{0,32},{8,40},{16,48},{24,56},{32,0},{40,8},{48,16},{56,24},{64,96... | collective-permute-start | bytes 417800 | tf_op jit(solution)/shard_map/ppermute | solution.py:110
  147.3 10.1 %collective-permute-start.13 = (f32[2,2,17,256]{3,1,2,0:T(2,128)S(1)}, f32[2,2,17,256]{3,1,2,0:T(2,128)S(1)}, u32[]{:S(2)}, u32[]{:S(2)}) collective-permute-start(f32[2,2,17,256]{3,1,2,0:T(2,128)S(1)} %bitcast.115), channel_id=1, source_target_pairs={{0,64},{8,72},{16,80},{24,88},{32,96},{40,104},{48,112},{56,120},{... | collective-permute-start | bytes 208904 | tf_op jit(solution)/shard_map/ppermute | solution.py:110
  157.5 5.8 %collective-permute-start.14 = (f32[2,17,256]{2,0,1:T(2,128)S(1)}, f32[2,17,256]{2,0,1:T(2,128)S(1)}, u32[]{:S(2)}, u32[]{:S(2)}) collective-permute-start(f32[2,17,256]{2,0,1:T(2,128)S(1)} %bitcast.116), channel_id=1, source_target_pairs={{0,128},{8,136},{16,144},{24,152},{32,160},{40,168},{48,176},{56,1... | collective-permute-start | bytes 104456 | tf_op jit(solution)/shard_map/ppermute | solution.py:110
  163.4 7.2 %collective-permute-start.15 = (f32[17,256]{1,0:T(8,128)S(1)}, f32[17,256]{1,0:T(8,128)S(1)}, u32[]{:S(2)}, u32[]{:S(2)}) collective-permute-start(f32[17,256]{1,0:T(8,128)S(1)} %bitcast.117), channel_id=1, source_target_pairs={{0,256},{8,264},{16,272},{24,280},{32,288},{40,296},{48,304},{56,3... | collective-permute-start | bytes 52232 | tf_op jit(solution)/shard_map/ppermute | solution.py:110
